TPU v7x, 256 devices: a whole 4x4x8 slice. The times are simulated.
256 devices in a mesh: act: 32 (over x, y, core), pix: 8 (over z).
Axes of the slice: x: 4, y: 4, z: 8, core: 2. Of those that a mesh axis runs over, the one named last changes fastest.
Arguments:
- pixel_index: int32 [8, 512], P('pix'), may hold values from 0 to 65535
- act_map: int32 [32768], P('act'), may hold values from 0 to 32767, each once
- omega: bfloat16 [32768, 128], P('act'), may hold values from -6 to 6
- pupil_field: float32 [8, 2, 32768], P('pix', None, 'act'), may hold values from -6 to 6
- channel_scale: float32 [8], P('pix'), may hold values from 0.9 to 1.1
- channel_flux: float32 [8], P('pix'), may hold values from 0.3 to 3
Outputs:
- basis_out: float32 [8, 1024, 128], P('pix', 'act')
- projection: float32 [128, 32768], P('pix', 'act')
- r_factor: float32 [128, 128], replicated
Inputs may be any that keep to these rules, and one draw needn't show every extreme that they name: `act_map`: every number of 0 to 32767 appears once. `pixel_index`: pixels of a channel may repeat.
All inputs are finite; a program needn't handle non-finite values.
Results may differ from a plain program's by a relative error of at most 0.0048.
Values may be sent and summed in bfloat16 or wider, within the bound.
No kernel may reach another device: no remote copies, remote signals or barrier semaphores. Data moves between devices by JAX's collectives and lax.ppermute only.
A program may use at most 64 MiB of HBM per device.

v0:
```python
import math
import jax
import jax.numpy as jnp
from jax import lax
from jax.sharding import PartitionSpec as P

GRID = 128
FOCAL = 256
RANK = 128
ACT = 32768
TWO_PI = 2.0 * math.pi
INFL_RATE = 4.5
DEFOCUS_RATE = 6.0


def jacobian_planes(pixels, wave_scale, flux_level, codes, field_re, field_im):
    delta_u = pixels // FOCAL - FOCAL // 2
    delta_v = pixels % FOCAL - FOCAL // 2
    mirror = codes // (GRID * GRID)
    column_x = codes // GRID % GRID - GRID // 2
    column_y = codes % GRID - GRID // 2
    phase_int = delta_u[:, None] * column_x[None, :] + delta_v[:, None] * column_y[None, :]
    radius = (delta_u * delta_u + delta_v * delta_v).astype(jnp.float32)
    amplitude = flux_level * jnp.exp(-INFL_RATE * radius / (FOCAL * FOCAL))
    defocus = radius * (TWO_PI * DEFOCUS_RATE / (FOCAL * FOCAL)) / wave_scale
    phase_angle = mirror.astype(jnp.float32)[None, :] * defocus[
        :, None
    ] - TWO_PI / FOCAL * wave_scale * phase_int.astype(jnp.float32)
    cosine = jnp.cos(phase_angle)
    sine_part = jnp.sin(phase_angle)
    real_part = amplitude[:, None] * (field_re[None, :] * cosine - field_im[None, :] * sine_part)
    imag_part = amplitude[:, None] * (field_re[None, :] * sine_part + field_im[None, :] * cosine)
    return (real_part.astype(jnp.bfloat16), imag_part.astype(jnp.bfloat16))


def gram_of(sketch):
    return lax.dot_general(
        sketch,
        sketch,
        (((0,), (0,)), ((), ())),
        precision=lax.Precision.HIGHEST,
        preferred_element_type=jnp.float32,
    )


def on_device(pixel_index, act_map, omega, pupil_field, channel_scale, channel_flux):
    pixels = pixel_index[0]
    npix = pixels.shape[0]
    rows_dev = 2 * npix
    act_count = lax.axis_size("act")
    pix_count = lax.axis_size("pix")
    total_rows = rows_dev * pix_count
    share_pix = npix // act_count
    real_rows, imag_rows = jacobian_planes(
        pixels, channel_scale[0], channel_flux[0], act_map, pupil_field[0, 0], pupil_field[0, 1]
    )
    jac = jnp.concatenate([real_rows, imag_rows], axis=0)
    partial_sketch = jnp.dot(jac, omega, preferred_element_type=jnp.float32)
    sketch = lax.psum(partial_sketch, "act")
    gram_matrix = lax.psum(gram_of(sketch), "pix")
    lower_factor = jnp.linalg.cholesky(gram_matrix)
    basis = jax.scipy.linalg.solve_triangular(lower_factor, sketch.T, lower=True).T
    first = lax.axis_index("act") * share_pix
    own_re = lax.dynamic_slice_in_dim(basis, first, share_pix, 0)
    own_im = lax.dynamic_slice_in_dim(basis, npix + first, share_pix, 0)
    own_basis = jnp.stack([own_re, own_im], axis=1).reshape(2 * share_pix, RANK)
    coarse = basis.astype(jnp.bfloat16)
    partial_value = lax.dot_general(
        coarse, jac, (((0,), (0,)), ((), ())), preferred_element_type=jnp.float32
    )
    projection = lax.psum_scatter(partial_value, "pix", scatter_dimension=0, tiled=True)
    basis_out = (own_basis * math.sqrt(total_rows)).reshape(1, 2 * share_pix, RANK)
    r_factor = lower_factor.T / math.sqrt(total_rows * ACT)
    return (basis_out, projection, r_factor)


def solution(mesh):
    return jax.shard_map(
        on_device,
        mesh=mesh,
        in_specs=(
            P("pix", None),
            P("act"),
            P("act", None),
            P("pix", None, "act"),
            P("pix"),
            P("pix"),
        ),
        out_specs=(P("pix", "act", None), P("pix", "act"), P()),
        check_vma=False,
    )
```

profile of v0, /device:TPU:2, one launch (start us, length us, event | category | flops | bytes accessed | tf_op | source)
XLA Modules:
  0.0 285.0 jit_solution(6364925790602597482)
XLA Ops:
  7.2 0.0 copy-start
  7.2 0.0 all-reduce.3.cloned.1.call-start
  7.9 0.7 fusion.16
  8.6 0.7 exponential_multiply_fusion
  10.0 0.7 fusion.9
  10.7 0.8 fusion.21
  11.4 0.7 multiply_divide_fusion
  12.1 9.1 %multiply_convert_fusion.1 = (bf16[512,1024]{1,0:T(8,128)(2,1)S(1)}, bf16[512,1024]{1,0:T(8,128)(2,1)S(1)}) fusion(f32[1024]{0:T(1024)S(1)} %bitcast.32, s32[1024]{0:T(1024)S(1)} %get-tuple-element.17, s32[512]{0:T(512)S(1)} %fusion.16, s32[1024]{0:T(1024)S(1)} %get-tuple-element.18, s32[512]{0:T(512)S(1)} %get-tuple-element.7, f32[]{:T(128)S(6)} %mul_shard_map.3, ...), kind=kLoop, calls=%fused_computation.2 | loop fusion | flops 8912896 | bytes 2125828 | tf_op jit(solution)/shard_map/convert_element_type | solution.py:33
  21.2 0.0 copy-done
  21.2 1.5 fusion.3
  22.7 0.0 all-reduce.3.cloned.1.call-update
  22.8 0.0 all-reduce.5.cloned.1.call-start
  22.8 116.9 %all-reduce.3.cloned.1.call-done = f32[1024,128]{1,0:T(8,128)} async-done(((f32[1024,128]{1,0:T(8,128)}), f32[1024,128]{1,0:T(8,128)}) %all-reduce.3.cloned.1.call-update) | async-done | bytes 524304 | tf_op jit(solution)/shard_map/psum | solution.py:59
  139.7 0.0 copy-start.1
  139.7 2.9 %fusion.22 = f32[128,128]{0,1:T(8,128)} fusion(f32[1024,128]{1,0:T(8,128)} %all-reduce.3.cloned.1.call-done), kind=kOutput, calls=%fused_computation.58 | convolution fusion | flops 201326592 | bytes 589824 | tf_op jit(solution)/shard_map/dot_general | solution.py:37
  142.6 0.0 all-reduce.5.cloned.1.call-update
  142.7 0.0 reduce-scatter.2.cloned.1.call-start
  142.7 72.8 %all-reduce.5.cloned.1.call-done = f32[128,128]{0,1:T(8,128)} async-done(((f32[128,128]{0,1:T(8,128)}), f32[128,128]{0,1:T(8,128)}) %all-reduce.5.cloned.1.call-update) | async-done | bytes 65552 | tf_op jit(solution)/shard_map/psum | solution.py:60
  215.5 0.9 copy.10
  216.4 0.9 fusion.7
  217.3 11.7 %cholesky.16 = f32[128,128]{1,0:T(8,128)S(1)} custom-call(f32[128,128]{1,0:T(8,128)S(1)} %fusion.7), custom_call_target="Cholesky" | custom-call | tf_op jit(solution)/shard_map/jit(cholesky)/cholesky | solution.py:61
  229.0 0.6 compare_reduce_fusion
  229.7 0.7 multiply_bitcast_fusion
  230.3 9.8 %custom-call.7 = f32[1,128,128]{1,2,0:T(8,128)S(1)} custom-call(f32[1,128,128]{2,1,0:T(8,128)S(1)} %get-tuple-element.11), custom_call_target="InvertDiagBlocksLowerTriangular" | custom-call | tf_op jit(solution)/shard_map/jit(_solve_triangular)/triangular_solve | solution.py:62
  240.1 0.0 copy-done.1
  240.1 0.6 fusion.5
  240.7 1.3 fusion.2
  242.0 0.0 reduce-scatter.2.cloned.1.call-update
  242.0 0.7 copy.11
  242.7 0.6 maximum_multiply_fusion
  243.4 35.1 %reduce-scatter.2.cloned.1.call-done = f32[16,1024]{1,0:T(8,128)} async-done(((f32[128,1024]{1,0:T(8,128)}), f32[16,1024]{1,0:T(8,128)}) %reduce-scatter.2.cloned.1.call-update) | async-done | bytes 65552 | tf_op jit(solution)/shard_map/reduce_scatter | solution.py:71
  (2 shorter events, 0.0 us)
Async XLA Ops:
  7.2 14.1 %copy-start = (bf16[1024,128]{1,0:T(8,128)(2,1)S(1)}, bf16[1024,128]{1,0:T(8,128)(2,1)}, u32[]{:S(2)}) copy-start(bf16[1024,128]{1,0:T(8,128)(2,1)} %param.8) | copy-start | bytes 786436
  7.2 132.6 %all-reduce.3.cloned.1.call-start = ((), (), s32[]{:S(2)}) async-start(), calls=%async_computation.1 | async-start | bytes 1048576 | tf_op jit(solution)/shard_map/psum | solution.py:59
  22.8 192.7 %all-reduce.5.cloned.1.call-start = ((), (), s32[]{:S(2)}) async-start(), calls=%async_computation.2 | async-start | bytes 131072 | tf_op jit(solution)/shard_map/psum | solution.py:60
  139.7 100.4 %copy-start.1 = (f32[1024,128]{1,0:T(8,128)S(1)}, f32[1024,128]{1,0:T(8,128)}, u32[]{:S(2)}) copy-start(f32[1024,128]{1,0:T(8,128)} %all-reduce.3.cloned.1.call-done) | copy-start | bytes 1572868
  142.7 135.8 %reduce-scatter.2.cloned.1.call-start = ((), (), s32[]{:S(2)}) async-start(), calls=%async_computation.3 | async-start | bytes 589824 | tf_op jit(solution)/shard_map/reduce_scatter | solution.py:71
Sparse Core Ops, SparseCore 0:
  22.9 116.8 all-reduce.2
  142.8 72.6 all-reduce.4
  242.1 36.2 reduce-scatter.1
where the time goes:
time: 285 us
  waiting for transfers between devices  225 us (79%)
  other arithmetic  36.2 us (13%)
  between operations  15.2 us (5%)
  matrix products  6.22 us (2%)
    psum x1, waiting for transfers between devices, on_device(): sketch = lax.psum(partial_sketch, 'act')  117 us
    psum x1, waiting for transfers between devices, on_device(): gram_matrix = lax.psum(gram_of(sketch), 'pix')  72.8 us
    reduce_scatter x1, waiting for transfers between devices, on_device(): lax.psum_scatter(partial_value, 'pix', scatter_dimension=0, tiled=True)  35.1 us
    another operation x3, other arithmetic, on_device(): lower_factor = jnp.linalg.cholesky(gram_matrix)  12.4 us
    another operation x1, other arithmetic, on_device(): jax.scipy.linalg.solve_triangular(lower_factor, sketch.T, lower=True)  9.81 us
    convert_element_type x1, other arithmetic, jacobian_planes(): return (real_part.astype(jnp.bfloat16), imag_part.astype(jnp.bfloat16))  9.06 us
  transfers between devices with their start and end apart: 3, of which 3 were waited for; matrix products, arithmetic and copies ran while one was open for 0% of the time, Pallas kernels for 0%

commit v1 on v0

--- a/solution.py
+++ b/solution.py
@@ -3,6 +3,7 @@
 import jax.numpy as jnp
 from jax import lax
 from jax.sharding import PartitionSpec as P
+from jax.lax import all_gather
 
 GRID = 128
 FOCAL = 256
@@ -57,7 +58,8 @@
     jac = jnp.concatenate([real_rows, imag_rows], axis=0)
     partial_sketch = jnp.dot(jac, omega, preferred_element_type=jnp.float32)
     sketch = lax.psum(partial_sketch, "act")
-    gram_matrix = lax.psum(gram_of(sketch), "pix")
+    block_here = gram_of(sketch)
+    gram_matrix = all_gather(block_here, axis_name="pix").sum(axis=0)
     lower_factor = jnp.linalg.cholesky(gram_matrix)
     basis = jax.scipy.linalg.solve_triangular(lower_factor, sketch.T, lower=True).T
     first = lax.axis_index("act") * share_pix

time: 285 us -> 237 us (0.83)
  waiting for transfers between devices: 225 us -> 152 us
  blocking collectives: 0 us -> 27.2 us
    psum x1 -> x0, waiting for transfers between devices: 72.8 us -> none  [on_device(): gram_matrix = lax.psum(gram_of(sketch), 'pix')]
    all_gather x0 -> x1, blocking collectives: none -> 27.2 us  [on_device(): gram_matrix = all_gather(block_here, axis_name='pix').sum(axis=0)]
  transfers between devices with their start and end apart: 3 -> 2, of which waited for: 3 -> 2; matrix products, arithmetic and copies ran while one was open for 0% -> 1% of each run, Pallas kernels for 0% -> 0%
where the time goes in v1:
time: 237 us
  waiting for transfers between devices  152 us (64%)
  other arithmetic  35.4 us (15%)
  blocking collectives  27.2 us (11%)
  between operations  15.5 us (7%)
  matrix products  5.54 us (2%)
    psum x1, waiting for transfers between devices, on_device(): sketch = lax.psum(partial_sketch, 'act')  117 us
    reduce_scatter x1, waiting for transfers between devices, on_device(): lax.psum_scatter(partial_value, 'pix', scatter_dimension=0, tiled=True)  34.8 us
    all_gather x1, blocking collectives, on_device(): gram_matrix = all_gather(block_here, axis_name='pix').sum(axis=0)  27.2 us
    another operation x3, other arithmetic, on_device(): lower_factor = jnp.linalg.cholesky(gram_matrix)  12.4 us
    another operation x1, other arithmetic, on_device(): jax.scipy.linalg.solve_triangular(lower_factor, sketch.T, lower=True)  9.81 us
    convert_element_type x1, other arithmetic, jacobian_planes(): return (real_part.astype(jnp.bfloat16), imag_part.astype(jnp.bfloat16))  9.06 us
  transfers between devices with their start and end apart: 2, of which 2 were waited for; matrix products, arithmetic and copies ran while one was open for 1% of the time, Pallas kernels for 0%

profile of v1, /device:TPU:2, one launch (start us, length us, event | category | flops | bytes accessed | tf_op | source)
XLA Modules:
  0.0 237.0 jit_solution(5964137047698215966)
XLA Ops:
  7.2 0.0 copy-start
  7.2 0.0 all-reduce.2.cloned.1.call-start
  7.9 0.7 fusion.16
  8.6 0.7 exponential_multiply_fusion
  10.0 0.7 fusion.9
  10.7 0.8 fusion.21
  11.4 0.7 multiply_divide_fusion
  12.1 9.1 %multiply_convert_fusion.1 = (bf16[512,1024]{1,0:T(8,128)(2,1)S(1)}, bf16[512,1024]{1,0:T(8,128)(2,1)S(1)}) fusion(f32[1024]{0:T(1024)S(1)} %bitcast.34, s32[1024]{0:T(1024)S(1)} %get-tuple-element.20, s32[512]{0:T(512)S(1)} %fusion.16, s32[1024]{0:T(1024)S(1)} %get-tuple-element.21, s32[512]{0:T(512)S(1)} %get-tuple-element.10, f32[]{:T(128)S(6)} %mul_shard_map.3, ...), kind=kLoop, calls=%fused_computation.2 | loop fusion | flops 8912896 | bytes 2125828 | tf_op jit(solution)/shard_map/convert_element_type | solution.py:34
  21.2 0.0 copy-done
  21.2 1.5 fusion.3
  22.7 0.0 all-reduce.2.cloned.1.call-update
  22.8 0.0 reduce-scatter.2.cloned.1.call-start
  22.8 116.9 %all-reduce.2.cloned.1.call-done = f32[1024,128]{1,0:T(8,128)} async-done(((f32[1024,128]{1,0:T(8,128)}), f32[1024,128]{1,0:T(8,128)}) %all-reduce.2.cloned.1.call-update) | async-done | bytes 524304 | tf_op jit(solution)/shard_map/psum | solution.py:60
  139.7 2.2 fusion.22
  141.9 0.0 copy-start.1
  142.0 27.2 %all-gather = f32[1024,128]{1,0:T(8,128)S(1)} all-gather(f32[128,128]{1,0:T(8,128)S(1)} %fusion.22), channel_id=2, replica_groups=mesh['act'=32,'pix'=8] {'pix'}, dimensions={0}, use_global_device_ids=true | all-gather | bytes 589824 | tf_op jit(solution)/shard_map/all_gather | solution.py:62
  169.2 0.1 copy.11
  169.3 11.7 %cholesky.16 = f32[128,128]{1,0:T(8,128)S(1)} custom-call(f32[128,128]{1,0:T(8,128)S(1)} %fusion.7), custom_call_target="Cholesky" | custom-call | tf_op jit(solution)/shard_map/jit(cholesky)/cholesky | solution.py:63
  181.1 0.6 compare_reduce_fusion
  181.7 0.7 multiply_bitcast_fusion
  182.4 9.8 %custom-call.7 = f32[1,128,128]{1,2,0:T(8,128)S(1)} custom-call(f32[1,128,128]{2,1,0:T(8,128)S(1)} %get-tuple-element.14), custom_call_target="InvertDiagBlocksLowerTriangular" | custom-call | tf_op jit(solution)/shard_map/jit(_solve_triangular)/triangular_solve | solution.py:64
  192.2 0.0 copy-done.1
  192.2 0.6 fusion.5
  192.8 1.3 fusion.2
  194.0 0.0 reduce-scatter.2.cloned.1.call-update
  194.1 0.7 copy.12
  194.8 0.6 maximum_multiply_fusion
  195.4 34.8 %reduce-scatter.2.cloned.1.call-done = f32[16,1024]{1,0:T(8,128)} async-done(((f32[128,1024]{1,0:T(8,128)}), f32[16,1024]{1,0:T(8,128)}) %reduce-scatter.2.cloned.1.call-update) | async-done | bytes 65552 | tf_op jit(solution)/shard_map/reduce_scatter | solution.py:73
  (4 shorter events, 0.1 us)
Async XLA Ops:
  7.2 14.1 %copy-start = (bf16[1024,128]{1,0:T(8,128)(2,1)S(1)}, bf16[1024,128]{1,0:T(8,128)(2,1)}, u32[]{:S(2)}) copy-start(bf16[1024,128]{1,0:T(8,128)(2,1)} %param.8) | copy-start | bytes 786436
  7.2 132.6 %all-reduce.2.cloned.1.call-start = ((), (), s32[]{:S(2)}) async-start(), calls=%async_computation.1 | async-start | bytes 1048576 | tf_op jit(solution)/shard_map/psum | solution.py:60
  22.8 207.4 %reduce-scatter.2.cloned.1.call-start = ((), (), s32[]{:S(2)}) async-start(), calls=%async_computation.2 | async-start | bytes 589824 | tf_op jit(solution)/shard_map/reduce_scatter | solution.py:73
  141.9 50.2 %copy-start.1 = (f32[1024,128]{1,0:T(8,128)S(1)}, f32[1024,128]{1,0:T(8,128)}, u32[]{:S(2)}) copy-start(f32[1024,128]{1,0:T(8,128)} %all-reduce.2.cloned.1.call-done) | copy-start | bytes 1572868
Sparse Core Ops, SparseCore 0:
  22.9 116.8 all-reduce.1
  194.2 35.9 reduce-scatter.1
